TPU v7x, 32 devices: a whole 2x2x4 slice. The times are simulated.
32 devices in a mesh: parts: 2 (over y), ctx: 8 (over z, x), tp: 2 (over core).
Axes of the slice: x: 2, y: 2, z: 4, core: 2. Of those that a mesh axis runs over, the one named last changes fastest.
Arguments:
- queries: bfloat16 [2048, 8192], P(('parts', 'ctx'), 'tp'), parts along dimension 0, may hold values from -9 to 9
- episode_key_cache: bfloat16 [128, 16, 1024], P(None, ('parts', 'ctx'), 'tp'), parts along dimension 1, may hold values from -9 to 9
- episode_value_cache: bfloat16 [128, 16, 1024], P(None, ('parts', 'ctx'), 'tp'), parts along dimension 1, may hold values from -6 to 6
- output_gradient: bfloat16 [2048, 8192], P(('parts', 'ctx'), 'tp'), parts along dimension 0, may hold values from -6 to 6
- block_lists: int32 [16, 2], P(('parts', 'ctx')), parts along dimension 0, may hold values from 0 to 7, as said below
- block_counts: int32 [16], P(('parts', 'ctx')), parts along dimension 0, may hold values from 1 to 2
Outputs:
- attn_out: bfloat16 [2048, 8192], P(('parts', 'ctx'), 'tp'), parts along dimension 0
- query_grad: bfloat16 [2048, 8192], P(('parts', 'ctx'), 'tp'), parts along dimension 0
- key_cache_gradient: bfloat16 [128, 16, 1024], P(None, ('parts', 'ctx'), 'tp'), parts along dimension 1
- value_cache_gradient: bfloat16 [128, 16, 1024], P(None, ('parts', 'ctx'), 'tp'), parts along dimension 1
There are 2 independent parts, one for each index of `parts`. A program takes and returns all parts, laid end to end along the dimension named above; each array names one. Nothing has to cross between parts.
Inputs may be any that keep to these rules, and one draw needn't show every extreme that they name: `block_lists`: each row names 2 different key blocks; a query block reads only its first block_counts entries.
All inputs are finite; a program needn't handle non-finite values.
Results may differ from a plain program's by a relative error of at most 0.0085.
The roundings to bfloat16 on the way count: a program that leaves them out, or rounds other values in their place, can miss the bound.
Values may be sent and summed in bfloat16 or wider, within the bound.
No kernel may reach another device: no remote copies, remote signals or barrier semaphores. Data moves between devices by JAX's collectives and lax.ppermute only.
A program may use at most 64 MiB of HBM per device.

v0:
```python
import jax
import jax.numpy as jnp
from jax import lax
from jax.sharding import PartitionSpec as P

QUERY_HEADS = 64
KEY_VALUE_HEADS = 8
HEAD_SIZE = 128
LIST = 2


def attend_group(query_part, key_part, value_part, grad_part, live_slots):
    score_scale = HEAD_SIZE ** (-0.5)
    scores = score_scale * jnp.einsum(
        "qah,jkh->aqjk", query_part, key_part, preferred_element_type=jnp.float32
    )
    masked = jnp.where(live_slots[None, None, :, None], scores, -jnp.inf)
    row_peak = jnp.max(masked, axis=(2, 3), keepdims=True)
    exponent = jnp.exp(masked - row_peak)
    weights = exponent / jnp.sum(exponent, axis=(2, 3), keepdims=True)
    weights_low = weights.astype(jnp.bfloat16)
    attended = jnp.einsum(
        "aqjk,jkh->qah", weights_low, value_part, preferred_element_type=jnp.float32
    ).astype(jnp.bfloat16)
    attended = lax.optimization_barrier(attended)
    row_delta = jnp.sum(grad_part.astype(jnp.float32) * attended.astype(jnp.float32), axis=2)
    weight_grad = jnp.einsum(
        "qah,jkh->aqjk", grad_part, value_part, preferred_element_type=jnp.float32
    )
    score_grad = (weights * (weight_grad - row_delta.T[:, :, None, None])).astype(jnp.bfloat16)
    query_grad = (
        score_scale
        * jnp.einsum("aqjk,jkh->qah", score_grad, key_part, preferred_element_type=jnp.float32)
    ).astype(jnp.bfloat16)
    key_piece = score_scale * jnp.einsum(
        "aqjk,qah->jkh", score_grad, query_part, preferred_element_type=jnp.float32
    )
    value_piece = jnp.einsum(
        "aqjk,qah->jkh", weights_low, grad_part, preferred_element_type=jnp.float32
    )
    return (attended, query_grad, key_piece, value_piece)


def arrange_rows(arrived):
    row_count, slot_count, peer_count, column_count = arrived.shape
    return jnp.transpose(arrived, (1, 2, 0, 3)).reshape(
        slot_count, peer_count * row_count, column_count
    )


def split_rows(pieces, row_count):
    slot_count, row_total, column_count = pieces.shape
    shaped = pieces.reshape(slot_count, row_total // row_count, row_count, column_count)
    return jnp.transpose(shaped, (2, 0, 1, 3))


def owner_sum(arrived, selector):
    summed = jnp.einsum("rjpc,jpn->rnc", arrived, selector, precision=lax.Precision.HIGHEST)
    return summed.astype(jnp.bfloat16)


def shards(
    queries, episode_key_cache, episode_value_cache, output_gradient, block_lists, block_counts
):
    held_keys, held_values = (
        lax.all_to_all(episode_key_cache, "ctx", split_axis=0, concat_axis=1, tiled=True),
        lax.all_to_all(episode_value_cache, "ctx", split_axis=0, concat_axis=1, tiled=True),
    )
    row_count = held_keys.shape[0]
    block_total = held_keys.shape[1]
    local_groups = held_keys.shape[2] // HEAD_SIZE
    queries_per_group = QUERY_HEADS // KEY_VALUE_HEADS
    query_rows = queries.shape[0]
    listed_all = lax.all_gather(block_lists, "ctx", axis=0, tiled=True)
    wanted = listed_all.T
    live_slots = jnp.arange(LIST, dtype=jnp.int32) < block_counts[0]
    selector = (
        wanted[:, :, None] == jnp.arange(block_total, dtype=jnp.int32)[None, None, :]
    ).astype(jnp.float32)
    picked_keys = jnp.take(held_keys, wanted, axis=1)
    picked_values = jnp.take(held_values, wanted, axis=1)

    def run_group(group_index, key_rows, value_rows):
        first_col = group_index * queries_per_group * HEAD_SIZE
        last_col = first_col + queries_per_group * HEAD_SIZE
        query_part = queries[:, first_col:last_col].reshape(
            query_rows, queries_per_group, HEAD_SIZE
        )
        grad_part = output_gradient[:, first_col:last_col].reshape(
            query_rows, queries_per_group, HEAD_SIZE
        )
        return attend_group(query_part, key_rows, value_rows, grad_part, live_slots)

    arrived_keys, arrived_values = (
        lax.all_to_all(picked_keys, "ctx", split_axis=2, concat_axis=2, tiled=True),
        lax.all_to_all(picked_values, "ctx", split_axis=2, concat_axis=2, tiled=True),
    )
    fetched_keys = arrange_rows(arrived_keys)
    fetched_values = arrange_rows(arrived_values)
    results = [
        run_group(
            group_index,
            fetched_keys[:, :, group_index * HEAD_SIZE : (group_index + 1) * HEAD_SIZE],
            fetched_values[:, :, group_index * HEAD_SIZE : (group_index + 1) * HEAD_SIZE],
        )
        for group_index in range(local_groups)
    ]
    key_pieces = jnp.concatenate([outcome[2] for outcome in results], axis=2)
    value_pieces = jnp.concatenate([outcome[3] for outcome in results], axis=2)
    back_keys, back_values = (
        lax.all_to_all(
            split_rows(key_pieces, row_count).astype(jnp.bfloat16),
            "ctx",
            split_axis=2,
            concat_axis=2,
            tiled=True,
        ).astype(jnp.float32),
        lax.all_to_all(
            split_rows(value_pieces, row_count).astype(jnp.bfloat16),
            "ctx",
            split_axis=2,
            concat_axis=2,
            tiled=True,
        ).astype(jnp.float32),
    )
    row_key_grad = owner_sum(back_keys, selector)
    row_value_grad = owner_sum(back_values, selector)
    key_cache_gradient, value_cache_gradient = (
        lax.all_to_all(row_key_grad, "ctx", split_axis=1, concat_axis=0, tiled=True),
        lax.all_to_all(row_value_grad, "ctx", split_axis=1, concat_axis=0, tiled=True),
    )
    attn_out = jnp.concatenate(
        [outcome[0].reshape(query_rows, queries_per_group * HEAD_SIZE) for outcome in results],
        axis=1,
    )
    query_grad = jnp.concatenate(
        [outcome[1].reshape(query_rows, queries_per_group * HEAD_SIZE) for outcome in results],
        axis=1,
    )
    return (attn_out, query_grad, key_cache_gradient, value_cache_gradient)


def solution(mesh):
    placed = (
        P(("parts", "ctx"), "tp"),
        P(None, ("parts", "ctx"), "tp"),
        P(None, ("parts", "ctx"), "tp"),
        P(("parts", "ctx"), "tp"),
        P(("parts", "ctx"), None),
        P(("parts", "ctx")),
    )
    return jax.shard_map(
        shards,
        mesh=mesh,
        in_specs=placed,
        out_specs=(
            P(("parts", "ctx"), "tp"),
            P(("parts", "ctx"), "tp"),
            P(None, ("parts", "ctx"), "tp"),
            P(None, ("parts", "ctx"), "tp"),
        ),
        check_vma=False,
    )
```

profile of v0, /device:TPU:0, one launch (start us, length us, event | category | flops | bytes accessed | tf_op | source)
XLA Modules:
  0.0 133.8 jit_solution(3935929716690283083)
XLA Ops:
  1.1 1.6 %reduce = bf16[128,512]{1,0:T(8,128)(2,1)S(1)} reduce(bf16[128,1,512]{2,0,1:T(8,128)(2,1)} %param.10, bf16[]{:T(256)} %broadcast.110), dimensions={1}, to_apply=%copy.184.reduce_sub_computation | reduce | bytes 262146 | tf_op args[2]
  3.5 7.3 %all-to-all-start = ((bf16[8,2,4096]{2,1,0:T(2,128)(2,1)}), bf16[8,2,4096]{2,1,0:T(2,128)(2,1)S(1)}, u32[]{:S(2)}, u32[]{:S(2)}) async-start(bf16[8,2,4096]{2,1,0:T(2,128)(2,1)} %reshape.189), calls=%async_computation | async-start | bytes 262144 | tf_op jit(solution)/shard_map/all_to_all | solution.py:67
  10.7 21.1 %all-gather = s32[8,1,2]{2,1,0:T(1,128)S(1)} all-gather(s32[1,1,2]{2,1,0:T(1,128)} %bitcast.467), channel_id=1, replica_groups=mesh['parts'=2,'ctx'=8,'tp'=2] {'ctx'}, dimensions={0}, use_global_device_ids=true | all-gather | bytes 72 | tf_op jit(solution)/shard_map/all_gather | solution.py:74
  32.1 1.6 %reduce.1 = bf16[128,512]{1,0:T(8,128)(2,1)S(1)} reduce(bf16[128,1,512]{2,0,1:T(8,128)(2,1)} %param.9, bf16[]{:T(256)} %broadcast.110), dimensions={1}, to_apply=%copy.188.reduce_sub_computation | reduce | bytes 262146 | tf_op args[1]
  34.4 3.4 %all-to-all-start.2 = ((bf16[8,2,4096]{2,1,0:T(2,128)(2,1)}), bf16[8,2,4096]{2,1,0:T(2,128)(2,1)S(1)}, u32[]{:S(2)}, u32[]{:S(2)}) async-start(bf16[8,2,4096]{2,1,0:T(2,128)(2,1)} %reshape.187), calls=%async_computation.2 | async-start | bytes 262144 | tf_op jit(solution)/shard_map/all_to_all | solution.py:66
  37.9 7.1 %all-to-all-done.2 = bf16[8,2,4096]{2,1,0:T(2,128)(2,1)S(1)} async-done(((bf16[8,2,4096]{2,1,0:T(2,128)(2,1)}), bf16[8,2,4096]{2,1,0:T(2,128)(2,1)S(1)}, u32[]{:S(2)}, u32[]{:S(2)}) %all-to-all-start.2) | async-done | bytes 131104 | tf_op jit(solution)/shard_map/all_to_all | solution.py:66
  47.2 3.4 %all-to-all-start.3 = ((bf16[16,2,8,512]{3,0,1,2:T(8,128)(2,1)}), bf16[16,2,8,512]{3,0,1,2:T(8,128)(2,1)S(1)}, u32[]{:S(2)}, u32[]{:S(2)}) async-start(bf16[16,2,8,512]{3,0,1,2:T(8,128)(2,1)} %copy.189), calls=%async_computation.3 | async-start | bytes 524288 | tf_op jit(solution)/shard_map/all_to_all | solution.py:95
  52.6 0.9 fusion.71
  53.5 1.2 copy.210
  56.6 2.2 %all-to-all-done.3 = bf16[16,2,8,512]{3,0,1,2:T(8,128)(2,1)S(1)} async-done(((bf16[16,2,8,512]{3,0,1,2:T(8,128)(2,1)}), bf16[16,2,8,512]{3,0,1,2:T(8,128)(2,1)S(1)}, u32[]{:S(2)}, u32[]{:S(2)}) %all-to-all-start.3) | async-done | bytes 262176 | tf_op jit(solution)/shard_map/all_to_all | solution.py:95
  58.8 4.0 %all-to-all-start.1 = ((bf16[16,2,8,512]{3,0,1,2:T(8,128)(2,1)}), bf16[16,2,8,512]{3,0,1,2:T(8,128)(2,1)}, u32[]{:S(2)}, u32[]{:S(2)}) async-start(bf16[16,2,8,512]{3,0,1,2:T(8,128)(2,1)} %copy.185), calls=%async_computation.1 | async-start | bytes 524288 | tf_op jit(solution)/shard_map/all_to_all | solution.py:96
  64.2 6.8 %all-to-all-done.1 = bf16[16,2,8,512]{3,0,1,2:T(8,128)(2,1)} async-done(((bf16[16,2,8,512]{3,0,1,2:T(8,128)(2,1)}), bf16[16,2,8,512]{3,0,1,2:T(8,128)(2,1)}, u32[]{:S(2)}, u32[]{:S(2)}) %all-to-all-start.1) | async-done | bytes 262176 | tf_op jit(solution)/shard_map/all_to_all | solution.py:96
  71.1 1.0 copy.186
  73.4 1.0 fusion.28
  76.8 0.9 fusion.30
  78.7 0.9 fusion.50
  83.1 2.0 %copy.239 = bf16[16,2,8,512]{3,1,0,2:T(2,128)(2,1)} copy(bf16[16,2,8,512]{3,0,2,1:T(8,128)(2,1)} %bitcast.447) | data formatting | bytes 524288 | tf_op jit(solution)/shard_map/convert_element_type | solution.py:112
  85.0 4.0 %all-to-all-start.4 = ((bf16[16,2,8,512]{3,1,0,2:T(2,128)(2,1)}), bf16[16,2,8,512]{3,1,0,2:T(2,128)(2,1)}, u32[]{:S(2)}, u32[]{:S(2)}) async-start(bf16[16,2,8,512]{3,1,0,2:T(2,128)(2,1)} %copy.239), calls=%async_computation.4 | async-start | bytes 524288 | tf_op jit(solution)/shard_map/all_to_all | solution.py:111
  89.1 1.0 fusion.29
  90.4 1.1 copy.231
  91.6 1.1 copy.232
  93.9 0.9 pad_maximum_fusion.3
  94.9 1.0 copy.247
  95.9 1.5 %all-to-all-done.4 = bf16[16,2,8,512]{3,1,0,2:T(2,128)(2,1)} async-done(((bf16[16,2,8,512]{3,1,0,2:T(2,128)(2,1)}), bf16[16,2,8,512]{3,1,0,2:T(2,128)(2,1)}, u32[]{:S(2)}, u32[]{:S(2)}) %all-to-all-start.4) | async-done | bytes 262176 | tf_op jit(solution)/shard_map/all_to_all | solution.py:111
  97.3 4.4 %all-to-all-start.6 = ((bf16[16,2,8,512]{3,1,0,2:T(2,128)(2,1)}), bf16[16,2,8,512]{3,1,0,2:T(2,128)(2,1)S(1)}, u32[]{:S(2)}, u32[]{:S(2)}) async-start(bf16[16,2,8,512]{3,1,0,2:T(2,128)(2,1)} %copy.247), calls=%async_computation.6 | async-start | bytes 524288 | tf_op jit(solution)/shard_map/all_to_all | solution.py:118
  102.3 1.2 fusion.39
  104.3 6.1 %all-to-all-done.6 = bf16[16,2,8,512]{3,1,0,2:T(2,128)(2,1)S(1)} async-done(((bf16[16,2,8,512]{3,1,0,2:T(2,128)(2,1)}), bf16[16,2,8,512]{3,1,0,2:T(2,128)(2,1)S(1)}, u32[]{:S(2)}, u32[]{:S(2)}) %all-to-all-start.6) | async-done | bytes 262176 | tf_op jit(solution)/shard_map/all_to_all | solution.py:118
  110.4 3.8 %all-to-all-start.5 = ((bf16[16,8,512]{2,0,1:T(8,128)(2,1)}), bf16[16,8,512]{2,0,1:T(8,128)(2,1)S(1)}, u32[]{:S(2)}, u32[]{:S(2)}) async-start(bf16[16,8,512]{2,0,1:T(8,128)(2,1)} %copy.241), calls=%async_computation.5 | async-start | bytes 262144 | tf_op jit(solution)/shard_map/all_to_all | solution.py:129
  115.2 6.5 %all-to-all-done.5 = bf16[16,8,512]{2,0,1:T(8,128)(2,1)S(1)} async-done(((bf16[16,8,512]{2,0,1:T(8,128)(2,1)}), bf16[16,8,512]{2,0,1:T(8,128)(2,1)S(1)}, u32[]{:S(2)}, u32[]{:S(2)}) %all-to-all-start.5) | async-done | bytes 131104 | tf_op jit(solution)/shard_map/all_to_all | solution.py:129
  121.8 3.4 %all-to-all-start.7 = ((bf16[16,8,512]{2,0,1:T(8,128)(2,1)}), bf16[16,8,512]{2,0,1:T(8,128)(2,1)S(1)}, u32[]{:S(2)}, u32[]{:S(2)}) async-start(bf16[16,8,512]{2,0,1:T(8,128)(2,1)} %copy.249), calls=%async_computation.7 | async-start | bytes 262144 | tf_op jit(solution)/shard_map/all_to_all | solution.py:130
  125.2 1.5 %pad_maximum_fusion = (bf16[128,4096]{1,0:T(8,128)(2,1)}, bf16[128,4096]{1,0:T(8,128)(2,1)}) fusion(bf16[128,1024]{1,0:T(8,128)(2,1)S(1)} %copy.209, bf16[128,1024]{1,0:T(8,128)(2,1)S(1)} %copy-done.7, bf16[128,1024]{1,0:T(8,128)(2,1)S(1)} %copy.207, bf16[128,1024]{1,0:T(8,128)(2,1)S(1)} %copy.206, bf16[128,1024]{1,0:T(8,128)(2,1)S(1)} %copy.233, ...), kind=kLoop, calls=%fused_computation.80 | loop fusion | flops 8388608 | bytes 4194304 | tf_op jit(solution)/shard_map/concatenate | solution.py:132
  126.7 5.8 %all-to-all-done.7 = bf16[16,8,512]{2,0,1:T(8,128)(2,1)S(1)} async-done(((bf16[16,8,512]{2,0,1:T(8,128)(2,1)}), bf16[16,8,512]{2,0,1:T(8,128)(2,1)S(1)}, u32[]{:S(2)}, u32[]{:S(2)}) %all-to-all-start.7) | async-done | bytes 131104 | tf_op jit(solution)/shard_map/all_to_all | solution.py:130
  (98 shorter events, 22.1 us)
Async XLA Ops:
  3.5 30.9 %all-to-all-start = ((bf16[8,2,4096]{2,1,0:T(2,128)(2,1)}), bf16[8,2,4096]{2,1,0:T(2,128)(2,1)S(1)}, u32[]{:S(2)}, u32[]{:S(2)}) async-start(bf16[8,2,4096]{2,1,0:T(2,128)(2,1)} %reshape.189), calls=%async_computation | async-start | bytes 262144 | tf_op jit(solution)/shard_map/all_to_all | solution.py:67
  34.4 10.7 %all-to-all-start.2 = ((bf16[8,2,4096]{2,1,0:T(2,128)(2,1)}), bf16[8,2,4096]{2,1,0:T(2,128)(2,1)S(1)}, u32[]{:S(2)}, u32[]{:S(2)}) async-start(bf16[8,2,4096]{2,1,0:T(2,128)(2,1)} %reshape.187), calls=%async_computation.2 | async-start | bytes 262144 | tf_op jit(solution)/shard_map/all_to_all | solution.py:66
  46.3 4.3 %copy-start.8 = (bf16[128,4096]{1,0:T(8,128)(2,1)S(1)}, bf16[128,4096]{1,0:T(8,128)(2,1)}, u32[]{:S(2)}) copy-start(bf16[128,4096]{1,0:T(8,128)(2,1)} %param.8) | copy-start | bytes 3145732
  47.2 11.6 %all-to-all-start.3 = ((bf16[16,2,8,512]{3,0,1,2:T(8,128)(2,1)}), bf16[16,2,8,512]{3,0,1,2:T(8,128)(2,1)S(1)}, u32[]{:S(2)}, u32[]{:S(2)}) async-start(bf16[16,2,8,512]{3,0,1,2:T(8,128)(2,1)} %copy.189), calls=%async_computation.3 | async-start | bytes 524288 | tf_op jit(solution)/shard_map/all_to_all | solution.py:95
  51.4 1.2 copy-start.9
  53.5 2.2 %copy-start.11 = (bf16[128,1024]{1,0:T(8,128)(2,1)S(1)}, bf16[128,1024]{1,0:T(8,128)(2,1)}, u32[]{:S(2)}) copy-start(bf16[128,1024]{1,0:T(8,128)(2,1)} %get-tuple-element.8) | copy-start | bytes 786436
  55.7 8.3 %copy-start.1 = (bf16[128,1024]{0,1:T(8,128)(2,1)}, bf16[128,1024]{0,1:T(8,128)(2,1)S(1)}, u32[]{:S(2)}) copy-start(bf16[128,1024]{0,1:T(8,128)(2,1)S(1)} %copy.225) | copy-start | bytes 786436
  58.8 12.3 %all-to-all-start.1 = ((bf16[16,2,8,512]{3,0,1,2:T(8,128)(2,1)}), bf16[16,2,8,512]{3,0,1,2:T(8,128)(2,1)}, u32[]{:S(2)}, u32[]{:S(2)}) async-start(bf16[16,2,8,512]{3,0,1,2:T(8,128)(2,1)} %copy.185), calls=%async_computation.1 | async-start | bytes 524288 | tf_op jit(solution)/shard_map/all_to_all | solution.py:96
  62.8 0.7 copy-start.3
  71.1 1.3 copy-start.2
  72.4 1.0 copy-start.4
  74.8 1.0 copy-start
  80.0 0.8 copy-start.5
  82.2 6.9 %copy-start.6 = (bf16[8,128,2,128]{1,3,0,2:T(8,128)(2,1)S(1)}, bf16[8,128,2,128]{1,3,0,2:T(8,128)(2,1)}, u32[]{:S(2)}) copy-start(bf16[8,128,2,128]{1,3,0,2:T(8,128)(2,1)} %copy-done.5) | copy-start | bytes 1572868
  83.1 7.0 %copy-start.10 = (bf16[128,8,128]{2,0,1:T(8,128)(2,1)S(1)}, bf16[128,8,128]{2,0,1:T(8,128)(2,1)}, u32[]{:S(2)}) copy-start(bf16[128,8,128]{2,0,1:T(8,128)(2,1)} %fusion.28) | copy-start | bytes 786436
  85.0 12.3 %all-to-all-start.4 = ((bf16[16,2,8,512]{3,1,0,2:T(2,128)(2,1)}), bf16[16,2,8,512]{3,1,0,2:T(2,128)(2,1)}, u32[]{:S(2)}, u32[]{:S(2)}) async-start(bf16[16,2,8,512]{3,1,0,2:T(2,128)(2,1)} %copy.239), calls=%async_computation.4 | async-start | bytes 524288 | tf_op jit(solution)/shard_map/all_to_all | solution.py:111
  97.3 13.1 %all-to-all-start.6 = ((bf16[16,2,8,512]{3,1,0,2:T(2,128)(2,1)}), bf16[16,2,8,512]{3,1,0,2:T(2,128)(2,1)S(1)}, u32[]{:S(2)}, u32[]{:S(2)}) async-start(bf16[16,2,8,512]{3,1,0,2:T(2,128)(2,1)} %copy.247), calls=%async_computation.6 | async-start | bytes 524288 | tf_op jit(solution)/shard_map/all_to_all | solution.py:118
  102.3 22.8 %copy-start.7 = (bf16[128,1024]{1,0:T(8,128)(2,1)S(1)}, bf16[128,1024]{1,0:T(8,128)(2,1)}, u32[]{:S(2)}) copy-start(bf16[128,1024]{1,0:T(8,128)(2,1)} %copy.208) | copy-start | bytes 786436
  110.4 11.3 %all-to-all-start.5 = ((bf16[16,8,512]{2,0,1:T(8,128)(2,1)}), bf16[16,8,512]{2,0,1:T(8,128)(2,1)S(1)}, u32[]{:S(2)}, u32[]{:S(2)}) async-start(bf16[16,8,512]{2,0,1:T(8,128)(2,1)} %copy.241), calls=%async_computation.5 | async-start | bytes 262144 | tf_op jit(solution)/shard_map/all_to_all | solution.py:129
  121.8 10.7 %all-to-all-start.7 = ((bf16[16,8,512]{2,0,1:T(8,128)(2,1)}), bf16[16,8,512]{2,0,1:T(8,128)(2,1)S(1)}, u32[]{:S(2)}, u32[]{:S(2)}) async-start(bf16[16,8,512]{2,0,1:T(8,128)(2,1)} %copy.249), calls=%async_computation.7 | async-start | bytes 262144 | tf_op jit(solution)/shard_map/all_to_all | solution.py:130
where the time goes:
time: 135 us; the launch traced here: 134 us
  waiting for transfers between devices  36 us (27%)
  starting transfers between devices  33.8 us (25%)
  local copies, waits for them, and re-layouts  22.3 us (17%)
  blocking collectives  21.1 us (16%)
  matrix products  11.2 us (8%)
  other arithmetic  7.34 us (5%)
  between operations  1.9 us (1%)
    all_gather x1, blocking collectives, shards(): listed_all = lax.all_gather(block_lists, 'ctx', axis=0, tiled=True)  21.1 us
    all_to_all x1, starting transfers between devices, shards(): lax.all_to_all(episode_value_cache, 'ctx', split_axis=0, concat_axis=1, t...  7.28 us
    all_to_all x1, waiting for transfers between devices, shards(): lax.all_to_all(episode_key_cache, 'ctx', split_axis=0, concat_axis=1, til...  7.1 us
    all_to_all x1, waiting for transfers between devices, shards(): lax.all_to_all(picked_values, 'ctx', split_axis=2, concat_axis=2, tiled=T...  6.83 us
    all_to_all x1, waiting for transfers between devices, shards(): lax.all_to_all(row_key_grad, 'ctx', split_axis=1, concat_axis=0, tiled=True)  6.53 us
    unnamed x37, local copies, waits for them, and re-layouts  6.16 us
    all_to_all x1, waiting for transfers between devices, shards(): lax.all_to_all(split_rows(value_pieces, row_count).astype(jnp.bfloat16),...  6.15 us
    all_to_all x1, waiting for transfers between devices, shards(): lax.all_to_all(row_value_grad, 'ctx', split_axis=1, concat_axis=0, tiled=...  5.78 us
  transfers between devices with their start and end apart: 8, of which 7 were waited for; matrix products, arithmetic and copies ran while one was open for 15% of the time, Pallas kernels for 0%

commit v1 on v0

--- a/solution.py
+++ b/solution.py
@@ -7,6 +7,27 @@
 KEY_VALUE_HEADS = 8
 HEAD_SIZE = 128
 LIST = 2
+
+
+def gather_around(x, axis, dim):
+    peers, index, rows = (lax.axis_size(axis), lax.axis_index(axis), x.shape[dim])
+    right = [(i, (i + 1) % peers) for i in range(peers)]
+    downward = [(i, (i - 1) % peers) for i in range(peers)]
+    out = jnp.zeros((*x.shape[:dim], peers * rows, *x.shape[dim + 1 :]), x.dtype)
+    out = lax.dynamic_update_slice_in_dim(out, x, index * rows, axis=dim)
+    from_left = from_right = x
+    half = peers // 2
+    for step in range(1, half + 1):
+        from_left = lax.ppermute(from_left, axis, right)
+        out = lax.dynamic_update_slice_in_dim(
+            out, from_left, (index - step) % peers * rows, axis=dim
+        )
+        if step < peers - half:
+            from_right = lax.ppermute(from_right, axis, downward)
+            out = lax.dynamic_update_slice_in_dim(
+                out, from_right, (index + step) % peers * rows, axis=dim
+            )
+    return out
 
 
 def attend_group(query_part, key_part, value_part, grad_part, live_slots):
@@ -71,7 +92,7 @@
     local_groups = held_keys.shape[2] // HEAD_SIZE
     queries_per_group = QUERY_HEADS // KEY_VALUE_HEADS
     query_rows = queries.shape[0]
-    listed_all = lax.all_gather(block_lists, "ctx", axis=0, tiled=True)
+    listed_all = gather_around(block_lists, "ctx", 0)
     wanted = listed_all.T
     live_slots = jnp.arange(LIST, dtype=jnp.int32) < block_counts[0]
     selector = (

time: 135 us -> 143 us (1.059)
  blocking collectives: 21.1 us -> 0 us
  waiting for transfers between devices: 36 us -> 53.2 us
  starting transfers between devices: 33.8 us -> 45.1 us
  local copies, waits for them, and re-layouts: 22.3 us -> 24.3 us
    all_gather x1 -> x0, blocking collectives: 21.1 us -> none  [shards(): listed_all = lax.all_gather(block_lists, 'ctx', axis=0, tiled=True)]
    ppermute x0 -> x7, waiting for transfers between devices: none -> 16.8 us  [the longest x4 16.8 us: gather_around(): from_left = lax.ppermute(from_left, axis, right)]
    ppermute x0 -> x7, starting transfers between devices: none -> 12.9 us  [the longest x3 10.9 us: gather_around(): from_right = lax.ppermute(from_right, axis, downward)]
    unnamed x37 -> x40, local copies, waits for them, and re-layouts: 6.16 us -> 6.9 us
  transfers between devices with their start and end apart: 8 -> 15, of which waited for: 7 -> 10; matrix products, arithmetic and copies ran while one was open for 15% -> 17% of each run, Pallas kernels for 0% -> 0%
where the time goes in v1:
time: 143 us; the launch traced here: 142 us
  waiting for transfers between devices  53.2 us (37%)
  starting transfers between devices  45.1 us (32%)
  local copies, waits for them, and re-layouts  24.3 us (17%)
  matrix products  11.2 us (8%)
  other arithmetic  6.43 us (4%)
  between operations  1.96 us (1%)
    ppermute x4, waiting for transfers between devices, gather_around(): from_left = lax.ppermute(from_left, axis, right)  16.8 us
    ppermute x3, starting transfers between devices, gather_around(): from_right = lax.ppermute(from_right, axis, downward)  10.9 us
    all_to_all x1, waiting for transfers between devices, shards(): lax.all_to_all(episode_key_cache, 'ctx', split_axis=0, concat_axis=1, til...  7.1 us
    unnamed x40, local copies, waits for them, and re-layouts  6.9 us
    all_to_all x1, waiting for transfers between devices, shards(): lax.all_to_all(picked_values, 'ctx', split_axis=2, concat_axis=2, tiled=T...  6.83 us
    all_to_all x1, waiting for transfers between devices, shards(): lax.all_to_all(split_rows(value_pieces, row_count).astype(jnp.bfloat16),...  6.73 us
    all_to_all x1, waiting for transfers between devices, shards(): lax.all_to_all(row_key_grad, 'ctx', split_axis=1, concat_axis=0, tiled=True)  6.31 us
    all_to_all x1, starting transfers between devices, shards(): lax.all_to_all(episode_value_cache, 'ctx', split_axis=0, concat_axis=1, t...  6 us
  transfers between devices with their start and end apart: 15, of which 10 were waited for; matrix products, arithmetic and copies ran while one was open for 17% of the time, Pallas kernels for 0%

profile of v1, /device:TPU:0, one launch (start us, length us, event | category | flops | bytes accessed | tf_op | source)
XLA Modules:
  0.0 142.2 jit_solution(10131388003164076226)
XLA Ops:
  0.6 6.1 %collective-permute-start.1 = (s32[1,2]{1,0:T(1,128)}, s32[1,2]{1,0:T(1,128)S(1)}, u32[]{:S(2)}, u32[]{:S(2)}) collective-permute-start(s32[1,2]{1,0:T(1,128)} %param.12), channel_id=1, source_target_pairs={{0,14},{2,0},{4,2},{6,4},{8,6},{10,8},{12,10},{14,12},{1,15},{3,1}... | collective-permute-start | bytes 32 | tf_op jit(solution)/shard_map/ppermute | solution.py:26
  7.2 1.6 %reduce = bf16[128,512]{1,0:T(8,128)(2,1)S(1)} reduce(bf16[128,1,512]{2,0,1:T(8,128)(2,1)} %param.10, bf16[]{:T(256)} %broadcast.121), dimensions={1}, to_apply=%copy.212.reduce_sub_computation | reduce | bytes 262146 | tf_op args[2]
  9.5 6.0 %all-to-all-start = ((bf16[8,2,4096]{2,1,0:T(2,128)(2,1)}), bf16[8,2,4096]{2,1,0:T(2,128)(2,1)S(1)}, u32[]{:S(2)}, u32[]{:S(2)}) async-start(bf16[8,2,4096]{2,1,0:T(2,128)(2,1)} %reshape.187), calls=%async_computation | async-start | bytes 262144 | tf_op jit(solution)/shard_map/all_to_all | solution.py:88
  18.1 4.8 %collective-permute-start.3 = (s32[1,2]{1,0:T(1,128)S(1)}, s32[1,2]{1,0:T(1,128)S(1)}, u32[]{:S(2)}, u32[]{:S(2)}) collective-permute-start(s32[1,2]{1,0:T(1,128)S(1)} %collective-permute-done.1), channel_id=1, source_target_pairs={{0,14},{2,0},{4,2},{6,4},{8,6},{10,8},{12,10},{14,12},{1,15},{3,1}... | collective-permute-start | bytes 32 | tf_op jit(solution)/shard_map/ppermute | solution.py:26
  22.9 6.3 %collective-permute-done.2 = s32[1,2]{1,0:T(1,128)S(1)} collective-permute-done((s32[1,2]{1,0:T(1,128)S(1)}, s32[1,2]{1,0:T(1,128)S(1)}, u32[]{:S(2)}, u32[]{:S(2)}) %collective-permute-start.2) | collective-permute-done | bytes 40 | tf_op jit(solution)/shard_map/ppermute | solution.py:21
  29.6 2.0 %collective-permute-start.4 = (s32[1,2]{1,0:T(1,128)S(1)}, s32[1,2]{1,0:T(1,128)S(1)}, u32[]{:S(2)}, u32[]{:S(2)}) collective-permute-start(s32[1,2]{1,0:T(1,128)S(1)} %collective-permute-done.2), channel_id=1, source_target_pairs={{0,2},{2,4},{4,6},{6,8},{8,10},{10,12},{12,14},{14,0},{1,3},{3,5},... | collective-permute-start | bytes 32 | tf_op jit(solution)/shard_map/ppermute | solution.py:21
  31.6 4.3 %collective-permute-done.4 = s32[1,2]{1,0:T(1,128)S(1)} collective-permute-done((s32[1,2]{1,0:T(1,128)S(1)}, s32[1,2]{1,0:T(1,128)S(1)}, u32[]{:S(2)}, u32[]{:S(2)}) %collective-permute-start.4) | collective-permute-done | bytes 40 | tf_op jit(solution)/shard_map/ppermute | solution.py:21
  36.3 6.3 %collective-permute-done.6 = s32[1,2]{1,0:T(1,128)S(1)} collective-permute-done((s32[1,2]{1,0:T(1,128)S(1)}, s32[1,2]{1,0:T(1,128)S(1)}, u32[]{:S(2)}, u32[]{:S(2)}) %collective-permute-start.6) | collective-permute-done | bytes 40 | tf_op jit(solution)/shard_map/ppermute | solution.py:21
  42.9 3.4 %all-to-all-start.2 = ((bf16[8,2,4096]{2,1,0:T(2,128)(2,1)}), bf16[8,2,4096]{2,1,0:T(2,128)(2,1)S(1)}, u32[]{:S(2)}, u32[]{:S(2)}) async-start(bf16[8,2,4096]{2,1,0:T(2,128)(2,1)} %reshape.185), calls=%async_computation.2 | async-start | bytes 262144 | tf_op jit(solution)/shard_map/all_to_all | solution.py:87
  46.4 7.1 %all-to-all-done.2 = bf16[8,2,4096]{2,1,0:T(2,128)(2,1)S(1)} async-done(((bf16[8,2,4096]{2,1,0:T(2,128)(2,1)}), bf16[8,2,4096]{2,1,0:T(2,128)(2,1)S(1)}, u32[]{:S(2)}, u32[]{:S(2)}) %all-to-all-start.2) | async-done | bytes 131104 | tf_op jit(solution)/shard_map/all_to_all | solution.py:87
  55.7 3.4 %all-to-all-start.3 = ((bf16[16,2,8,512]{3,0,1,2:T(8,128)(2,1)}), bf16[16,2,8,512]{3,0,1,2:T(8,128)(2,1)S(1)}, u32[]{:S(2)}, u32[]{:S(2)}) async-start(bf16[16,2,8,512]{3,0,1,2:T(8,128)(2,1)} %copy.217), calls=%async_computation.3 | async-start | bytes 524288 | tf_op jit(solution)/shard_map/all_to_all | solution.py:116
  62.0 1.2 copy.238
  65.1 2.2 %all-to-all-done.3 = bf16[16,2,8,512]{3,0,1,2:T(8,128)(2,1)S(1)} async-done(((bf16[16,2,8,512]{3,0,1,2:T(8,128)(2,1)}), bf16[16,2,8,512]{3,0,1,2:T(8,128)(2,1)S(1)}, u32[]{:S(2)}, u32[]{:S(2)}) %all-to-all-start.3) | async-done | bytes 262176 | tf_op jit(solution)/shard_map/all_to_all | solution.py:116
  67.3 4.1 %all-to-all-start.1 = ((bf16[16,2,8,512]{3,0,1,2:T(8,128)(2,1)}), bf16[16,2,8,512]{3,0,1,2:T(8,128)(2,1)}, u32[]{:S(2)}, u32[]{:S(2)}) async-start(bf16[16,2,8,512]{3,0,1,2:T(8,128)(2,1)} %copy.213), calls=%async_computation.1 | async-start | bytes 524288 | tf_op jit(solution)/shard_map/all_to_all | solution.py:117
  72.8 6.8 %all-to-all-done.1 = bf16[16,2,8,512]{3,0,1,2:T(8,128)(2,1)} async-done(((bf16[16,2,8,512]{3,0,1,2:T(8,128)(2,1)}), bf16[16,2,8,512]{3,0,1,2:T(8,128)(2,1)}, u32[]{:S(2)}, u32[]{:S(2)}) %all-to-all-start.1) | async-done | bytes 262176 | tf_op jit(solution)/shard_map/all_to_all | solution.py:117
  79.6 1.0 copy.214
  81.9 1.0 fusion.28
  91.6 2.0 %copy.267 = bf16[16,2,8,512]{3,1,0,2:T(2,128)(2,1)} copy(bf16[16,2,8,512]{3,0,2,1:T(8,128)(2,1)} %bitcast.444) | data formatting | bytes 524288 | tf_op jit(solution)/shard_map/convert_element_type | solution.py:133
  93.6 4.2 %all-to-all-start.4 = ((bf16[16,2,8,512]{3,1,0,2:T(2,128)(2,1)}), bf16[16,2,8,512]{3,1,0,2:T(2,128)(2,1)}, u32[]{:S(2)}, u32[]{:S(2)}) async-start(bf16[16,2,8,512]{3,1,0,2:T(2,128)(2,1)} %copy.267), calls=%async_computation.4 | async-start | bytes 524288 | tf_op jit(solution)/shard_map/all_to_all | solution.py:132
  97.8 1.0 fusion.29
  99.1 1.1 copy.259
  100.3 1.1 copy.260
  103.6 1.0 copy.275
  104.6 1.4 all-to-all-done.4
  106.0 4.3 %all-to-all-start.6 = ((bf16[16,2,8,512]{3,1,0,2:T(2,128)(2,1)}), bf16[16,2,8,512]{3,1,0,2:T(2,128)(2,1)S(1)}, u32[]{:S(2)}, u32[]{:S(2)}) async-start(bf16[16,2,8,512]{3,1,0,2:T(2,128)(2,1)} %copy.275), calls=%async_computation.6 | async-start | bytes 524288 | tf_op jit(solution)/shard_map/all_to_all | solution.py:139
  110.9 1.2 fusion.39
  112.8 6.7 %all-to-all-done.6 = bf16[16,2,8,512]{3,1,0,2:T(2,128)(2,1)S(1)} async-done(((bf16[16,2,8,512]{3,1,0,2:T(2,128)(2,1)}), bf16[16,2,8,512]{3,1,0,2:T(2,128)(2,1)S(1)}, u32[]{:S(2)}, u32[]{:S(2)}) %all-to-all-start.6) | async-done | bytes 262176 | tf_op jit(solution)/shard_map/all_to_all | solution.py:139
  119.6 3.4 %all-to-all-start.5 = ((bf16[16,8,512]{2,0,1:T(8,128)(2,1)}), bf16[16,8,512]{2,0,1:T(8,128)(2,1)S(1)}, u32[]{:S(2)}, u32[]{:S(2)}) async-start(bf16[16,8,512]{2,0,1:T(8,128)(2,1)} %copy.269), calls=%async_computation.5 | async-start | bytes 262144 | tf_op jit(solution)/shard_map/all_to_all | solution.py:150
  123.9 6.3 %all-to-all-done.5 = bf16[16,8,512]{2,0,1:T(8,128)(2,1)S(1)} async-done(((bf16[16,8,512]{2,0,1:T(8,128)(2,1)}), bf16[16,8,512]{2,0,1:T(8,128)(2,1)S(1)}, u32[]{:S(2)}, u32[]{:S(2)}) %all-to-all-start.5) | async-done | bytes 131104 | tf_op jit(solution)/shard_map/all_to_all | solution.py:150
  130.2 3.4 %all-to-all-start.7 = ((bf16[16,8,512]{2,0,1:T(8,128)(2,1)}), bf16[16,8,512]{2,0,1:T(8,128)(2,1)S(1)}, u32[]{:S(2)}, u32[]{:S(2)}) async-start(bf16[16,8,512]{2,0,1:T(8,128)(2,1)} %copy.277), calls=%async_computation.7 | async-start | bytes 262144 | tf_op jit(solution)/shard_map/all_to_all | solution.py:151
  133.6 1.5 %pad_maximum_fusion = (bf16[128,4096]{1,0:T(8,128)(2,1)}, bf16[128,4096]{1,0:T(8,128)(2,1)}) fusion(bf16[128,1024]{1,0:T(8,128)(2,1)S(1)} %copy.237, bf16[128,1024]{1,0:T(8,128)(2,1)S(1)} %copy-done.7, bf16[128,1024]{1,0:T(8,128)(2,1)S(1)} %copy.235, bf16[128,1024]{1,0:T(8,128)(2,1)S(1)} %copy.234, bf16[128,1024]{1,0:T(8,128)(2,1)S(1)} %copy.261, ...), kind=kLoop, calls=%fused_computation.80 | loop fusion | flops 8388608 | bytes 4194304 | tf_op jit(solution)/shard_map/concatenate | solution.py:153
  135.1 5.8 %all-to-all-done.7 = bf16[16,8,512]{2,0,1:T(8,128)(2,1)S(1)} async-done(((bf16[16,8,512]{2,0,1:T(8,128)(2,1)}), bf16[16,8,512]{2,0,1:T(8,128)(2,1)S(1)}, u32[]{:S(2)}, u32[]{:S(2)}) %all-to-all-start.7) | async-done | bytes 131104 | tf_op jit(solution)/shard_map/all_to_all | solution.py:151
  (129 shorter events, 28.5 us)
Async XLA Ops:
  0.6 15.6 %copy-start.12 = (bf16[128,1,512]{2,0,1:T(8,128)(2,1)S(1)}, bf16[128,1,512]{2,0,1:T(8,128)(2,1)}, u32[]{:S(2)}) copy-start(bf16[128,1,512]{2,0,1:T(8,128)(2,1)} %param.9) | copy-start | bytes 393220
  0.6 17.3 %collective-permute-start.1 = (s32[1,2]{1,0:T(1,128)}, s32[1,2]{1,0:T(1,128)S(1)}, u32[]{:S(2)}, u32[]{:S(2)}) collective-permute-start(s32[1,2]{1,0:T(1,128)} %param.12), channel_id=1, source_target_pairs={{0,14},{2,0},{4,2},{6,4},{8,6},{10,8},{12,10},{14,12},{1,15},{3,1}... | collective-permute-start | bytes 32 | tf_op jit(solution)/shard_map/ppermute | solution.py:26
  6.7 11.0 %collective-permute-start = (s32[1,2]{1,0:T(1,128)}, s32[1,2]{1,0:T(1,128)S(1)}, u32[]{:S(2)}, u32[]{:S(2)}) collective-permute-start(s32[1,2]{1,0:T(1,128)} %param.12), channel_id=1, source_target_pairs={{0,2},{2,4},{4,6},{6,8},{8,10},{10,12},{12,14},{14,0},{1,3},{3,5},... | collective-permute-start | bytes 32 | tf_op jit(solution)/shard_map/ppermute | solution.py:21
  9.5 33.3 %all-to-all-start = ((bf16[8,2,4096]{2,1,0:T(2,128)(2,1)}), bf16[8,2,4096]{2,1,0:T(2,128)(2,1)S(1)}, u32[]{:S(2)}, u32[]{:S(2)}) async-start(bf16[8,2,4096]{2,1,0:T(2,128)(2,1)} %reshape.187), calls=%async_computation | async-start | bytes 262144 | tf_op jit(solution)/shard_map/all_to_all | solution.py:88
  18.1 11.2 %collective-permute-start.3 = (s32[1,2]{1,0:T(1,128)S(1)}, s32[1,2]{1,0:T(1,128)S(1)}, u32[]{:S(2)}, u32[]{:S(2)}) collective-permute-start(s32[1,2]{1,0:T(1,128)S(1)} %collective-permute-done.1), channel_id=1, source_target_pairs={{0,14},{2,0},{4,2},{6,4},{8,6},{10,8},{12,10},{14,12},{1,15},{3,1}... | collective-permute-start | bytes 32 | tf_op jit(solution)/shard_map/ppermute | solution.py:26
  22.9 6.3 %collective-permute-start.2 = (s32[1,2]{1,0:T(1,128)S(1)}, s32[1,2]{1,0:T(1,128)S(1)}, u32[]{:S(2)}, u32[]{:S(2)}) collective-permute-start(s32[1,2]{1,0:T(1,128)S(1)} %collective-permute-done), channel_id=1, source_target_pairs={{0,2},{2,4},{4,6},{6,8},{8,10},{10,12},{12,14},{14,0},{1,3},{3,5},... | collective-permute-start | bytes 32 | tf_op jit(solution)/shard_map/ppermute | solution.py:21
  29.5 6.6 %collective-permute-start.5 = (s32[1,2]{1,0:T(1,128)S(1)}, s32[1,2]{1,0:T(1,128)S(1)}, u32[]{:S(2)}, u32[]{:S(2)}) collective-permute-start(s32[1,2]{1,0:T(1,128)S(1)} %collective-permute-done.3), channel_id=1, source_target_pairs={{0,14},{2,0},{4,2},{6,4},{8,6},{10,8},{12,10},{14,12},{1,15},{3,1}... | collective-permute-start | bytes 32 | tf_op jit(solution)/shard_map/ppermute | solution.py:26
  29.6 6.3 %collective-permute-start.4 = (s32[1,2]{1,0:T(1,128)S(1)}, s32[1,2]{1,0:T(1,128)S(1)}, u32[]{:S(2)}, u32[]{:S(2)}) collective-permute-start(s32[1,2]{1,0:T(1,128)S(1)} %collective-permute-done.2), channel_id=1, source_target_pairs={{0,2},{2,4},{4,6},{6,8},{8,10},{10,12},{12,14},{14,0},{1,3},{3,5},... | collective-permute-start | bytes 32 | tf_op jit(solution)/shard_map/ppermute | solution.py:21
  36.3 6.3 %collective-permute-start.6 = (s32[1,2]{1,0:T(1,128)S(1)}, s32[1,2]{1,0:T(1,128)S(1)}, u32[]{:S(2)}, u32[]{:S(2)}) collective-permute-start(s32[1,2]{1,0:T(1,128)S(1)} %collective-permute-done.4), channel_id=1, source_target_pairs={{0,2},{2,4},{4,6},{6,8},{8,10},{10,12},{12,14},{14,0},{1,3},{3,5},... | collective-permute-start | bytes 32 | tf_op jit(solution)/shard_map/ppermute | solution.py:21
  42.9 10.7 %all-to-all-start.2 = ((bf16[8,2,4096]{2,1,0:T(2,128)(2,1)}), bf16[8,2,4096]{2,1,0:T(2,128)(2,1)S(1)}, u32[]{:S(2)}, u32[]{:S(2)}) async-start(bf16[8,2,4096]{2,1,0:T(2,128)(2,1)} %reshape.185), calls=%async_computation.2 | async-start | bytes 262144 | tf_op jit(solution)/shard_map/all_to_all | solution.py:87
  54.8 4.3 %copy-start.8 = (bf16[128,4096]{1,0:T(8,128)(2,1)S(1)}, bf16[128,4096]{1,0:T(8,128)(2,1)}, u32[]{:S(2)}) copy-start(bf16[128,4096]{1,0:T(8,128)(2,1)} %param.8) | copy-start | bytes 3145732
  55.7 11.6 %all-to-all-start.3 = ((bf16[16,2,8,512]{3,0,1,2:T(8,128)(2,1)}), bf16[16,2,8,512]{3,0,1,2:T(8,128)(2,1)S(1)}, u32[]{:S(2)}, u32[]{:S(2)}) async-start(bf16[16,2,8,512]{3,0,1,2:T(8,128)(2,1)} %copy.217), calls=%async_computation.3 | async-start | bytes 524288 | tf_op jit(solution)/shard_map/all_to_all | solution.py:116
  59.9 1.2 copy-start.9
  62.0 2.2 %copy-start.11 = (bf16[128,1024]{1,0:T(8,128)(2,1)S(1)}, bf16[128,1024]{1,0:T(8,128)(2,1)}, u32[]{:S(2)}) copy-start(bf16[128,1024]{1,0:T(8,128)(2,1)} %get-tuple-element.8) | copy-start | bytes 786436
  64.1 8.3 %copy-start.1 = (bf16[128,1024]{0,1:T(8,128)(2,1)}, bf16[128,1024]{0,1:T(8,128)(2,1)S(1)}, u32[]{:S(2)}) copy-start(bf16[128,1024]{0,1:T(8,128)(2,1)S(1)} %copy.253) | copy-start | bytes 786436
  67.3 12.3 %all-to-all-start.1 = ((bf16[16,2,8,512]{3,0,1,2:T(8,128)(2,1)}), bf16[16,2,8,512]{3,0,1,2:T(8,128)(2,1)}, u32[]{:S(2)}, u32[]{:S(2)}) async-start(bf16[16,2,8,512]{3,0,1,2:T(8,128)(2,1)} %copy.213), calls=%async_computation.1 | async-start | bytes 524288 | tf_op jit(solution)/shard_map/all_to_all | solution.py:117
  71.4 0.7 copy-start.3
  79.6 1.3 copy-start.2
  81.0 1.0 copy-start.4
  83.3 1.0 copy-start
  88.6 0.8 copy-start.5
  90.7 7.1 %copy-start.6 = (bf16[8,128,2,128]{1,3,0,2:T(8,128)(2,1)S(1)}, bf16[8,128,2,128]{1,3,0,2:T(8,128)(2,1)}, u32[]{:S(2)}) copy-start(bf16[8,128,2,128]{1,3,0,2:T(8,128)(2,1)} %copy-done.5) | copy-start | bytes 1572868
  91.6 7.2 %copy-start.10 = (bf16[128,8,128]{2,0,1:T(8,128)(2,1)S(1)}, bf16[128,8,128]{2,0,1:T(8,128)(2,1)}, u32[]{:S(2)}) copy-start(bf16[128,8,128]{2,0,1:T(8,128)(2,1)} %fusion.28) | copy-start | bytes 786436
  93.6 12.4 %all-to-all-start.4 = ((bf16[16,2,8,512]{3,1,0,2:T(2,128)(2,1)}), bf16[16,2,8,512]{3,1,0,2:T(2,128)(2,1)}, u32[]{:S(2)}, u32[]{:S(2)}) async-start(bf16[16,2,8,512]{3,1,0,2:T(2,128)(2,1)} %copy.267), calls=%async_computation.4 | async-start | bytes 524288 | tf_op jit(solution)/shard_map/all_to_all | solution.py:132
  106.0 13.6 %all-to-all-start.6 = ((bf16[16,2,8,512]{3,1,0,2:T(2,128)(2,1)}), bf16[16,2,8,512]{3,1,0,2:T(2,128)(2,1)S(1)}, u32[]{:S(2)}, u32[]{:S(2)}) async-start(bf16[16,2,8,512]{3,1,0,2:T(2,128)(2,1)} %copy.275), calls=%async_computation.6 | async-start | bytes 524288 | tf_op jit(solution)/shard_map/all_to_all | solution.py:139
  110.9 22.7 %copy-start.7 = (bf16[128,1024]{1,0:T(8,128)(2,1)S(1)}, bf16[128,1024]{1,0:T(8,128)(2,1)}, u32[]{:S(2)}) copy-start(bf16[128,1024]{1,0:T(8,128)(2,1)} %copy.236) | copy-start | bytes 786436
  119.6 10.7 %all-to-all-start.5 = ((bf16[16,8,512]{2,0,1:T(8,128)(2,1)}), bf16[16,8,512]{2,0,1:T(8,128)(2,1)S(1)}, u32[]{:S(2)}, u32[]{:S(2)}) async-start(bf16[16,8,512]{2,0,1:T(8,128)(2,1)} %copy.269), calls=%async_computation.5 | async-start | bytes 262144 | tf_op jit(solution)/shard_map/all_to_all | solution.py:150
  130.2 10.7 %all-to-all-start.7 = ((bf16[16,8,512]{2,0,1:T(8,128)(2,1)}), bf16[16,8,512]{2,0,1:T(8,128)(2,1)S(1)}, u32[]{:S(2)}, u32[]{:S(2)}) async-start(bf16[16,8,512]{2,0,1:T(8,128)(2,1)} %copy.277), calls=%async_computation.7 | async-start | bytes 262144 | tf_op jit(solution)/shard_map/all_to_all | solution.py:151
